TPU v7x, 256 devices: a whole 4x4x8 slice. The times are simulated.
256 devices in a mesh: row: 4 (over z_lo), col: 64 (over y, x, z_hi, core).
Axes of the slice: x: 4, y: 4, z: 8 (z_hi: 2, z_lo: 4; z = z_hi * 4 + z_lo), core: 2. Of those that a mesh axis runs over, the one named last changes fastest.
Arguments:
- iterate: float32 [256, 131072], P('row', 'col'), may hold values from -6 to 6
- residual: float32 [256, 131072], P('row', 'col'), may hold values from -24 to 24
- direction: float32 [256, 131072], P('row', 'col'), may hold values from -24 to 24
- window_weight: float32 [16, 8192], P('row', 'col'), may hold values from 0.2 to 5
- freq_weight: float32 [32, 32], replicated, may hold values from 0.2 to 5
Outputs:
- new_iterate: float32 [256, 131072], P('row', 'col')
- new_residual: float32 [256, 131072], P('row', 'col')
- new_direction: float32 [256, 131072], P('row', 'col')
All inputs are finite; a program needn't handle non-finite values.
Results may differ from a plain program's by a relative error of at most 0.0003.
Values sent between devices are 32-bit elements; how exact they have to be, the bound alone decides.
No kernel may reach another device: no remote copies, remote signals or barrier semaphores. Data moves between devices by JAX's collectives and lax.ppermute only.
A program may use at most 64 MiB of HBM per device.

v0:
```python
import jax
import jax.numpy as jnp
from jax import lax
from jax.sharding import Mesh
from jax.sharding import PartitionSpec as P

COL = ("col_0", "col_1", "col_2", "col_3")
ROW_COL = ("row", "col_0", "col_1", "col_2", "col_3")
precise = lax.Precision.HIGHEST
damping = 0.5


def passed_along(value, axis, steps):
    count = lax.axis_size(axis)
    leading, last = (max(0, -steps), min(count, count - steps))
    return lax.ppermute(value, axis, [(source, source + steps) for source in range(leading, last)])


def over_axes(x, axes):
    for axis in axes:
        x = lax.psum(x, axis)
    return x


def tables():
    positions = jnp.arange(32, dtype=jnp.float32)
    window = jnp.exp(-0.5 * ((positions - 15.5) / 8.0) ** 2)
    phases = 2.0 * jnp.pi * jnp.outer(positions, positions) / 32.0
    cos_part = jnp.cos(phases) * window[None, :] / jnp.sqrt(32.0)
    sin_part = -jnp.sin(phases) * window[None, :] / jnp.sqrt(32.0)
    column_table = jnp.concatenate([cos_part.T, sin_part.T], axis=1)
    cos_split = cos_part.reshape(32, 2, 16)
    sin_split = sin_part.reshape(32, 2, 16)
    upper = jnp.stack([cos_split, -sin_split], axis=-1)
    lower = jnp.stack([sin_split, cos_split], axis=-1)
    row_table = jnp.concatenate([upper, lower], axis=0).reshape(64, 64)
    return (column_table, row_table)


def analyze(region, column_table, row_table):
    win_rows = region.shape[0] // 16 - 1
    win_cols = region.shape[1] // 16 - 1
    blocks = region.reshape(win_rows + 1, 16, win_cols + 1, 16)
    section_one = jnp.einsum(
        "akbl,lp->akpb", blocks[:, :, :win_cols], column_table[:16], precision=precise
    )
    section_one = section_one + jnp.einsum(
        "akbl,lp->akpb", blocks[:, :, 1:], column_table[16:], precision=precise
    )
    section_one = section_one.reshape(win_rows + 1, 16, 2, 32, win_cols)
    paired = jnp.stack([section_one[:-1], section_one[1:]], axis=1).reshape(
        win_rows, 64, 32, win_cols
    )
    return jnp.einsum("tm,amvb->atvb", row_table, paired, precision=precise)


def weigh(coefficients, window_weight, freq_weight):
    doubled = jnp.concatenate([freq_weight, freq_weight], axis=0)
    return coefficients * doubled[None, :, :, None] * window_weight[:, None, None, :]


def synthesize(coefficients, column_table, row_table):
    win_rows = coefficients.shape[0]
    win_cols = coefficients.shape[3]
    spread = jnp.einsum("tm,atvb->amvb", row_table, coefficients, precision=precise)
    spread = spread.reshape(win_rows, 2, 16, 64, win_cols)
    stacked = jnp.pad(spread[:, 0], ((0, 1), (0, 0), (0, 0), (0, 0))) + jnp.pad(
        spread[:, 1], ((1, 0), (0, 0), (0, 0), (0, 0))
    )
    lower_piece = jnp.einsum("akpb,lp->akbl", stacked, column_table[:16], precision=precise)
    upper_piece = jnp.einsum("akpb,lp->akbl", stacked, column_table[16:], precision=precise)
    blocks = jnp.pad(lower_piece, ((0, 0), (0, 0), (0, 1), (0, 0))) + jnp.pad(
        upper_piece, ((0, 0), (0, 0), (1, 0), (0, 0))
    )
    return blocks.reshape(16 * (win_rows + 1), 16 * (win_cols + 1))


def per_device(iterate, residual, direction, window_weight, freq_weight):
    column_table, row_table = tables()
    height, breadth = direction.shape
    beside = passed_along(direction[:, :16], COL, -1)
    widened = jnp.concatenate([direction, beside], axis=1)
    below = passed_along(widened[:16], "row", -1)
    region = jnp.concatenate([widened, below], axis=0)
    coefficients = weigh(analyze(region, column_table, row_table), window_weight, freq_weight)
    spread = synthesize(coefficients, column_table, row_table)
    arrived_rows = passed_along(spread[height:], "row", 1)
    upper_rows = jnp.concatenate([spread[:16] + arrived_rows, spread[16:height]], axis=0)
    arrived_cols = passed_along(upper_rows[:, breadth:], COL, 1)
    synthesized = jnp.concatenate(
        [upper_rows[:, :16] + arrived_cols, upper_rows[:, 16:breadth]], axis=1
    )
    applied = synthesized + damping * direction
    norm_now, curvature, cross_term, image_norm = (
        over_axes(jnp.sum(residual * residual), ROW_COL),
        over_axes(jnp.sum(direction * applied), ROW_COL),
        over_axes(jnp.sum(residual * applied), ROW_COL),
        over_axes(jnp.sum(applied * applied), ROW_COL),
    )
    step_length = norm_now / curvature
    new_iterate = iterate + step_length * direction
    new_residual = residual - step_length * applied
    norm_next = norm_now - 2.0 * step_length * cross_term + step_length * step_length * image_norm
    new_direction = new_residual + norm_next / norm_now * direction
    return (new_iterate, new_residual, new_direction)


def solution(mesh):
    finer = Mesh(
        mesh.devices.reshape(mesh.shape["row"], 4, 4, 2, 2),
        ("row", "col_0", "col_1", "col_2", "col_3"),
    )
    return jax.shard_map(
        per_device,
        mesh=finer,
        in_specs=(P("row", COL), P("row", COL), P("row", COL), P("row", COL), P()),
        out_specs=(P("row", COL), P("row", COL), P("row", COL)),
        check_vma=False,
    )
```

profile of v0, /device:TPU:1, one launch (start us, length us, event | category | flops | bytes accessed | tf_op | source)
XLA Modules:
  0.0 132.1 jit_solution(15178026938067578234)
XLA Ops:
  0.6 0.8 slice.62
  1.4 5.1 %collective-permute-start = (f32[64,16]{1,0:T(8,128)S(1)}, f32[64,16]{1,0:T(8,128)S(1)}, u32[]{:S(2)}, u32[]{:S(2)}) collective-permute-start(f32[64,16]{1,0:T(8,128)S(1)} %slice.62), channel_id=1, source_target_pairs={{1,0},{2,1},{3,2},{4,3},{5,4},{6,5},{7,6},{8,7},{9,8},{10,9},{11,1... | collective-permute-start | bytes 12296 | tf_op jit(solution)/shard_map/ppermute | solution.py:16
  6.6 1.1 constant_dynamic-update-slice_fusion.1
  7.7 0.1 multiply_multiply_fusion.4
  7.7 0.1 fusion.26
  7.9 0.8 pad_maximum_fusion.2
  8.7 4.5 %collective-permute-done = f32[64,16]{1,0:T(8,128)S(1)} collective-permute-done((f32[64,16]{1,0:T(8,128)S(1)}, f32[64,16]{1,0:T(8,128)S(1)}, u32[]{:S(2)}, u32[]{:S(2)}) %collective-permute-start) | collective-permute-done | bytes 4128 | tf_op jit(solution)/shard_map/ppermute | solution.py:16
  13.2 1.3 collective-permute-start.1
  14.5 0.1 maximum_maximum_fusion
  14.6 0.1 copy.31
  14.7 0.1 fusion.25
  14.7 4.3 %collective-permute-done.1 = f32[16,2064]{1,0:T(8,128)S(1)} collective-permute-done((f32[16,2064]{1,0:T(8,128)S(1)}, f32[16,2064]{1,0:T(8,128)S(1)}, u32[]{:S(2)}, u32[]{:S(2)}) %collective-permute-start.1) | collective-permute-done | bytes 132128 | tf_op jit(solution)/shard_map/ppermute | solution.py:16
  19.0 3.2 %reshape.132 = f32[5,16,129,16]{3,2,1,0:T(8,128)} reshape(f32[80,2064]{1,0:T(8,128)S(1)} %pad_maximum_fusion) | data formatting | bytes 1320960 | tf_op jit(solution)/shard_map/reshape | solution.py:43
  22.3 8.1 %fusion = f32[64,5,16,128]{3,0,2,1:T(8,128)S(1)} fusion(f32[16,64,1,1]{1,0,3,2:T(8,128)S(1)} %fusion.25, f32[5,16,129,16]{3,2,1,0:T(8,128)} %reshape.132), kind=kOutput, calls=%fused_computation | convolution fusion | flops 125829120 | bytes 7868416 | tf_op jit(solution)/shard_map/akbl,lp->akpb/dot_general | solution.py:47
  30.4 0.0 copy-done
  30.4 5.8 %add_bitcast_fusion = f32[5,16,64,128]{3,2,1,0:T(8,128)S(1)} fusion(f32[64,5,16,128]{3,0,2,1:T(8,128)S(1)} %fusion, f32[5,16,129,16]{3,2,1,0:T(8,128)S(1)} %copy-done, f32[32,32]{1,0:T(8,128)S(1)} %get-tuple-element.40, f32[32,32]{1,0:T(8,128)S(1)} %get-tuple-element.41), kind=kOutput, calls=%fused_computation.12 | convolution fusion | flops 126485504 | bytes 10518528 | tf_op jit(solution)/shard_map/akbl,lp->akpb/dot_general | solution.py:44
  36.2 0.6 fusion.35
  36.8 1.2 copy.29
  38.1 1.2 copy.30
  39.3 0.0 copy-start.4
  39.3 4.2 %fusion.4 = f32[4,32,128,64,1,1]{2,3,5,4,1,0:T(8,128)S(1)} fusion(f32[4,1,16,2,32,128]{5,2,3,1,4,0:T(8,128)S(1)} %copy.30, f32[4,1,16,2,32,128]{5,2,3,1,4,0:T(8,128)S(1)} %copy.29, f32[64,2,16,2]{0,2,3,1:T(8,128)S(1)} %maximum_maximum_fusion), kind=kOutput, calls=%fused_computation.4 | convolution fusion | flops 806354944 | bytes 8404992 | tf_op jit(solution)/shard_map/tm,amvb->atvb/dot_general | solution.py:54
  43.5 4.4 %fusion.11 = f32[4,64,32,128]{3,1,2,0:T(8,128)S(1)} fusion(f32[64,64,1,1]{0,1,3,2:T(8,128)S(1)} %bitcast.50, f32[4,32,128,64,1,1]{2,3,5,4,1,0:T(8,128)S(1)} %fusion.4, f32[4,128]{1,0:T(4,128)S(1)} %copy-done.4, f32[64,32]{0,1:T(8,128)S(1)} %copy.31), kind=kOutput, calls=%fused_computation.13 | convolution fusion | flops 807403520 | bytes 8415232 | tf_op jit(solution)/shard_map/tm,atvb->amvb/dot_general | solution.py:65
  47.9 2.4 %copy.33 = f32[4,64,32,128]{3,2,1,0:T(8,128)S(1)} copy(f32[4,64,32,128]{3,1,2,0:T(8,128)S(1)} %fusion.11) | data formatting | bytes 8388608 | tf_op jit(solution)/shard_map/tm,atvb->amvb/transpose | solution.py:65
  50.3 0.6 slice_bitcast_fusion.1
  50.9 1.5 %fusion.19 = f32[5,16,128,16]{2,3,1,0:T(8,128)S(1)} fusion(f32[4,16,64,128]{3,2,1,0:T(8,128)S(1)} %get-tuple-element.31, f32[4,16,64,128]{3,2,1,0:T(8,128)S(1)} %get-tuple-element.30, f32[32,32]{1,0:T(8,128)S(1)} %get-tuple-element.40, f32[32,32]{1,0:T(8,128)S(1)} %get-tuple-element.41), kind=kOutput, calls=%fused_computation.19 | convolution fusion | flops 126485504 | bytes 4857856 | tf_op jit(solution)/shard_map/akpb,lp->akbl/dot_general | solution.py:70
  52.4 1.5 %fusion.18 = f32[5,16,128,16]{2,3,1,0:T(8,128)S(1)} fusion(f32[16,64,1,1]{1,0,3,2:T(8,128)S(1)} %fusion.25, f32[4,16,64,128]{3,2,1,0:T(8,128)S(1)} %get-tuple-element.31, f32[4,16,64,128]{3,2,1,0:T(8,128)S(1)} %get-tuple-element.30), kind=kOutput, calls=%fused_computation.18 | convolution fusion | flops 126484480 | bytes 4853760 | tf_op jit(solution)/shard_map/akpb,lp->akbl/dot_general | solution.py:71
  53.9 0.2 pad_add_fusion.4
  54.1 0.4 copy.36
  54.5 1.0 slice.74
  55.5 3.4 %collective-permute-start.2 = (f32[16,2064]{1,0:T(8,128)}, f32[16,2064]{1,0:T(8,128)}, u32[]{:S(2)}, u32[]{:S(2)}) collective-permute-start(f32[16,2064]{1,0:T(8,128)} %slice.74), channel_id=1, source_target_pairs={{0,64},{64,128},{128,192},{1,65},{65,129},{129,193},{2,66},{66,130... | collective-permute-start | bytes 396296 | tf_op jit(solution)/shard_map/ppermute | solution.py:16
  58.9 0.4 copy.35
  59.3 0.3 slice.72
  59.6 1.1 pad_add_fusion.3
  60.7 2.1 %copy.37 = f32[3,16,129,16]{3,2,1,0:T(8,128)S(1)} copy(f32[3,16,129,16]{2,3,1,0:T(8,128)} %pad_add_fusion.3) | data formatting | bytes 792576 | tf_op jit(solution)/shard_map/slice | solution.py:88
  62.8 1.6 %slice.76 = f32[48,2064]{1,0:T(8,128)} reshape(f32[3,16,129,16]{3,2,1,0:T(8,128)S(1)} %copy.37) | data formatting | bytes 792576 | tf_op jit(solution)/shard_map/slice | solution.py:88
  64.5 0.0 collective-permute-done.2
  64.5 1.0 add.98
  65.5 0.7 pad_maximum_fusion.1
  66.2 3.8 %collective-permute-start.3 = (f32[64,16]{1,0:T(8,128)S(1)}, f32[64,16]{1,0:T(8,128)S(1)}, u32[]{:S(2)}, u32[]{:S(2)}) collective-permute-start(f32[64,16]{1,0:T(8,128)S(1)} %pad_maximum_fusion.1), channel_id=1, source_target_pairs={{0,1},{1,2},{2,3},{3,4},{4,5},{5,6},{6,7},{7,8},{8,9},{9,10},{10,1... | collective-permute-start | bytes 12296 | tf_op jit(solution)/shard_map/ppermute | solution.py:16
  70.1 1.0 collective-permute-done.3
  71.1 0.7 maximum_add_fusion
  71.8 2.1 %multiply_reduce_fusion = (f32[]{:T(128)}, f32[]{:T(128)}, f32[]{:T(128)}, f32[]{:T(128)}, f32[64,2048]{1,0:T(8,128)S(1)}) fusion(f32[64,2048]{1,0:T(8,128)} %param.6, f32[64,2048]{1,0:T(8,128)} %param.7, f32[48,2064]{1,0:T(8,128)} %slice.76, f32[16,2064]{1,0:T(8,128)S(1)} %add.98, f32[64,16]{1,0:T(8,128)S(1)} %maximum_add_fusion), kind=kLoop, calls=%fused_computation.27 | loop fusion | flops 1966076 | bytes 2105360 | tf_op jit(solution)/shard_map/reduce_sum | solution.py:98
  73.9 7.4 %all-reduce.6 = (f32[]{:T(128)}, f32[]{:T(128)}, f32[]{:T(128)}, f32[]{:T(128)}) all-reduce(f32[]{:T(128)} %get-tuple-element.5, f32[]{:T(128)} %get-tuple-element.6, f32[]{:T(128)} %get-tuple-element.4, f32[]{:T(128)} %get-tuple-element.3), channel_id=1, replica_groups=mesh['row'=4,'col_0'=4,'col_1'=4,'col_2'=2,'col_3'=2] {'row'}, use_global_device_ids=true, to_apply=%region_1.2 | all-reduce | flops 4 | bytes 32 | tf_op jit(solution)/shard_map/psum | solution.py:21
  81.3 11.2 %all-reduce.5 = (f32[]{:T(128)}, f32[]{:T(128)}, f32[]{:T(128)}, f32[]{:T(128)}) all-reduce(f32[]{:T(128)} %get-tuple-element.15, f32[]{:T(128)} %get-tuple-element.16, f32[]{:T(128)} %get-tuple-element.17, f32[]{:T(128)} %get-tuple-element.18), channel_id=1, replica_groups=mesh['row'=4,'col_0'=4,'col_1'=4,'col_2'=2,'col_3'=2] {'col_0'}, use_global_device_ids=true, to_apply=%region_2.3 | all-reduce | flops 4 | bytes 32 | tf_op jit(solution)/shard_map/psum | solution.py:21
  92.6 8.9 %all-reduce.4 = (f32[]{:T(128)}, f32[]{:T(128)}, f32[]{:T(128)}, f32[]{:T(128)}) all-reduce(f32[]{:T(128)} %get-tuple-element.11, f32[]{:T(128)} %get-tuple-element.12, f32[]{:T(128)} %get-tuple-element.13, f32[]{:T(128)} %get-tuple-element.14), channel_id=1, replica_groups=mesh['row'=4,'col_0'=4,'col_1'=4,'col_2'=2,'col_3'=2] {'col_1'}, use_global_device_ids=true, to_apply=%region_3.4 | all-reduce | flops 4 | bytes 32 | tf_op jit(solution)/shard_map/psum | solution.py:21
  101.5 8.3 %all-reduce.8 = (f32[]{:T(128)}, f32[]{:T(128)}, f32[]{:T(128)}, f32[]{:T(128)}) all-reduce(f32[]{:T(128)} %get-tuple-element.7, f32[]{:T(128)} %get-tuple-element.8, f32[]{:T(128)} %get-tuple-element.9, f32[]{:T(128)} %get-tuple-element.10), channel_id=1, replica_groups=mesh['row'=4,'col_0'=4,'col_1'=4,'col_2'=2,'col_3'=2] {'col_2'}, use_global_device_ids=true, to_apply=%region_4.5 | all-reduce | flops 4 | bytes 32 | tf_op jit(solution)/shard_map/psum | solution.py:21
  109.8 17.1 %all-reduce.7 = (f32[]{:T(128)}, f32[]{:T(128)}, f32[]{:T(128)}, f32[]{:T(128)}) all-reduce(f32[]{:T(128)} %get-tuple-element.23, f32[]{:T(128)} %get-tuple-element.24, f32[]{:T(128)} %get-tuple-element.25, f32[]{:T(128)} %get-tuple-element.26), channel_id=1, replica_groups=mesh['row'=4,'col_0'=4,'col_1'=4,'col_2'=2,'col_3'=2] {'col_3'}, use_global_device_ids=true, to_apply=%region_5.6 | all-reduce | flops 4 | bytes 32 | tf_op jit(solution)/shard_map/psum | solution.py:21
  130.9 1.2 multiply_add_fusion
  (14 shorter events, 0.1 us)
Async XLA Ops:
  1.4 11.8 %collective-permute-start = (f32[64,16]{1,0:T(8,128)S(1)}, f32[64,16]{1,0:T(8,128)S(1)}, u32[]{:S(2)}, u32[]{:S(2)}) collective-permute-start(f32[64,16]{1,0:T(8,128)S(1)} %slice.62), channel_id=1, source_target_pairs={{1,0},{2,1},{3,2},{4,3},{5,4},{6,5},{7,6},{8,7},{9,8},{10,9},{11,1... | collective-permute-start | bytes 12296 | tf_op jit(solution)/shard_map/ppermute | solution.py:16
  13.2 5.8 %collective-permute-start.1 = (f32[16,2064]{1,0:T(8,128)S(1)}, f32[16,2064]{1,0:T(8,128)S(1)}, u32[]{:S(2)}, u32[]{:S(2)}) collective-permute-start(f32[16,2064]{1,0:T(8,128)S(1)} %slice.82), channel_id=1, source_target_pairs={{64,0},{128,64},{192,128},{65,1},{129,65},{193,129},{66,2},{130,66... | collective-permute-start | bytes 396296 | tf_op jit(solution)/shard_map/ppermute | solution.py:16
  22.3 8.1 %copy-start = (f32[5,16,129,16]{3,2,1,0:T(8,128)S(1)}, f32[5,16,129,16]{3,2,1,0:T(8,128)}, u32[]{:S(2)}) copy-start(f32[5,16,129,16]{3,2,1,0:T(8,128)} %reshape.132) | copy-start | bytes 1981444
  39.3 4.2 %copy-start.4 = (f32[4,128]{1,0:T(4,128)S(1)}, f32[4,128]{1,0:T(4,128)}, u32[]{:S(2)}) copy-start(f32[4,128]{1,0:T(4,128)} %param.8) | copy-start | bytes 6148
  55.5 8.9 %collective-permute-start.2 = (f32[16,2064]{1,0:T(8,128)}, f32[16,2064]{1,0:T(8,128)}, u32[]{:S(2)}, u32[]{:S(2)}) collective-permute-start(f32[16,2064]{1,0:T(8,128)} %slice.74), channel_id=1, source_target_pairs={{0,64},{64,128},{128,192},{1,65},{65,129},{129,193},{2,66},{66,130... | collective-permute-start | bytes 396296 | tf_op jit(solution)/shard_map/ppermute | solution.py:16
  64.4 66.4 %copy-start.1 = (f32[64,2048]{1,0:T(8,128)S(1)}, f32[64,2048]{1,0:T(8,128)}, u32[]{:S(2)}) copy-start(f32[64,2048]{1,0:T(8,128)} %param.7) | copy-start | bytes 1572868
  64.4 66.4 %copy-start.2 = (f32[64,2048]{1,0:T(8,128)S(1)}, f32[64,2048]{1,0:T(8,128)}, u32[]{:S(2)}) copy-start(f32[64,2048]{1,0:T(8,128)} %param.6) | copy-start | bytes 1572868
  64.4 66.5 %copy-start.3 = (f32[64,2048]{1,0:T(8,128)S(1)}, f32[64,2048]{1,0:T(8,128)}, u32[]{:S(2)}) copy-start(f32[64,2048]{1,0:T(8,128)} %param.5) | copy-start | bytes 1572868
  66.2 4.8 %collective-permute-start.3 = (f32[64,16]{1,0:T(8,128)S(1)}, f32[64,16]{1,0:T(8,128)S(1)}, u32[]{:S(2)}, u32[]{:S(2)}) collective-permute-start(f32[64,16]{1,0:T(8,128)S(1)} %pad_maximum_fusion.1), channel_id=1, source_target_pairs={{0,1},{1,2},{2,3},{3,4},{4,5},{5,6},{6,7},{7,8},{8,9},{9,10},{10,1... | collective-permute-start | bytes 12296 | tf_op jit(solution)/shard_map/ppermute | solution.py:16
where the time goes:
time: 133 us; the launch traced here: 132 us
  blocking collectives  52.9 us (40%)
  matrix products  25.5 us (19%)
  local copies, waits for them, and re-layouts  17 us (13%)
  starting transfers between devices  13.6 us (10%)
  waiting for transfers between devices  9.75 us (7%)
  other arithmetic  8.5 us (6%)
  between operations  4.85 us (4%)
    psum x5, blocking collectives, over_axes(): x = lax.psum(x, axis)  52.9 us
    ppermute x4, starting transfers between devices, passed_along(): lax.ppermute(value, axis, [(source, source + steps) for source in range(l...  13.6 us
    ppermute x4, waiting for transfers between devices, passed_along(): lax.ppermute(value, axis, [(source, source + steps) for source in range(l...  9.75 us
    dot_general x1, matrix products, analyze(): jnp.einsum('akbl,lp->akpb', blocks[:, :, 1:], column_table[16:], precisio...  8.08 us
    dot_general x1, matrix products, analyze(): jnp.einsum('akbl,lp->akpb', blocks[:, :, :win_cols], column_table[:16], p...  5.81 us
    dot_general x1, matrix products, synthesize(): jnp.einsum('tm,atvb->amvb', row_table, coefficients, precision=precise)  4.37 us
    dot_general x1, matrix products, analyze(): return jnp.einsum('tm,amvb->atvb', row_table, paired, precision=precise)  4.16 us
    slice x2, local copies, waits for them, and re-layouts, per_device(): spread[16:height]  3.69 us
  transfers between devices with their start and end apart: 4, of which 3 were waited for; matrix products, arithmetic and copies ran while one was open for 6% of the time, Pallas kernels for 0%

commit v1 on v0

--- a/solution.py
+++ b/solution.py
@@ -18,7 +18,8 @@
 
 def over_axes(x, axes):
     for axis in axes:
-        x = lax.psum(x, axis)
+        parts = lax.all_gather(x, axis)
+        x = jnp.sum(parts, axis=0)
     return x
 
 

time: 133 us -> 172 us (1.29)
  local copies, waits for them, and re-layouts: 17 us -> 48.1 us
  other arithmetic: 8.5 us -> 20.5 us
  blocking collectives: 52.9 us -> 49.5 us
    psum x5 -> x0, blocking collectives: 52.9 us -> none  [over_axes(): x = lax.psum(x, axis)]
    unnamed x0 -> x5, blocking collectives: none -> 49.5 us
    unnamed x11 -> x66, local copies, waits for them, and re-layouts: 1.1 us -> 32.3 us
    reduce_sum x0 -> x20, other arithmetic: none -> 12 us  [over_axes(): x = jnp.sum(parts, axis=0)]
  transfers between devices with their start and end apart: 4 -> 4, of which waited for: 3 -> 3; matrix products, arithmetic and copies ran while one was open for 6% -> 5% of each run, Pallas kernels for 0% -> 0%
where the time goes in v1:
time: 172 us; the launch traced here: 171 us
  blocking collectives  49.5 us (29%)
  local copies, waits for them, and re-layouts  48.1 us (28%)
  matrix products  25.5 us (15%)
  other arithmetic  20.5 us (12%)
  starting transfers between devices  13.6 us (8%)
  waiting for transfers between devices  9.07 us (5%)
  between operations  4.91 us (3%)
    unnamed x5, blocking collectives  49.5 us
    unnamed x66, local copies, waits for them, and re-layouts  32.3 us
    ppermute x4, starting transfers between devices, passed_along(): lax.ppermute(value, axis, [(source, source + steps) for source in range(l...  13.6 us
    reduce_sum x20, other arithmetic, over_axes(): x = jnp.sum(parts, axis=0)  12 us
    ppermute x4, waiting for transfers between devices, passed_along(): lax.ppermute(value, axis, [(source, source + steps) for source in range(l...  9.07 us
    dot_general x1, matrix products, analyze(): jnp.einsum('akbl,lp->akpb', blocks[:, :, 1:], column_table[16:], precisio...  8.1 us
    dot_general x1, matrix products, analyze(): jnp.einsum('akbl,lp->akpb', blocks[:, :, :win_cols], column_table[:16], p...  5.8 us
    dot_general x1, matrix products, synthesize(): jnp.einsum('tm,atvb->amvb', row_table, coefficients, precision=precise)  4.38 us
  transfers between devices with their start and end apart: 4, of which 3 were waited for; matrix products, arithmetic and copies ran while one was open for 5% of the time, Pallas kernels for 0%

profile of v1, /device:TPU:1, one launch (start us, length us, event | category | flops | bytes accessed | tf_op | source)
XLA Modules:
  0.0 171.3 jit_solution(4003012283849033373)
XLA Ops:
  1.4 5.1 %collective-permute-start = (f32[64,16]{1,0:T(8,128)S(1)}, f32[64,16]{1,0:T(8,128)S(1)}, u32[]{:S(2)}, u32[]{:S(2)}) collective-permute-start(f32[64,16]{1,0:T(8,128)S(1)} %slice.62), channel_id=1, source_target_pairs={{1,0},{2,1},{3,2},{4,3},{5,4},{6,5},{7,6},{8,7},{9,8},{10,9},{11,1... | collective-permute-start | bytes 12296 | tf_op jit(solution)/shard_map/ppermute | solution.py:16
  6.6 1.1 constant_dynamic-update-slice_fusion.1
  8.7 4.5 %collective-permute-done = f32[64,16]{1,0:T(8,128)S(1)} collective-permute-done((f32[64,16]{1,0:T(8,128)S(1)}, f32[64,16]{1,0:T(8,128)S(1)}, u32[]{:S(2)}, u32[]{:S(2)}) %collective-permute-start) | collective-permute-done | bytes 4128 | tf_op jit(solution)/shard_map/ppermute | solution.py:16
  13.2 1.3 collective-permute-start.1
  14.7 4.3 %collective-permute-done.1 = f32[16,2064]{1,0:T(8,128)S(1)} collective-permute-done((f32[16,2064]{1,0:T(8,128)S(1)}, f32[16,2064]{1,0:T(8,128)S(1)}, u32[]{:S(2)}, u32[]{:S(2)}) %collective-permute-start.1) | collective-permute-done | bytes 132128 | tf_op jit(solution)/shard_map/ppermute | solution.py:16
  19.0 3.2 %reshape.132 = f32[5,16,129,16]{3,2,1,0:T(8,128)} reshape(f32[80,2064]{1,0:T(8,128)S(1)} %pad_maximum_fusion) | data formatting | bytes 1320960 | tf_op jit(solution)/shard_map/reshape | solution.py:44
  22.3 8.1 %fusion = f32[64,5,16,128]{3,0,2,1:T(8,128)S(1)} fusion(f32[16,64,1,1]{1,0,3,2:T(8,128)S(1)} %fusion.25, f32[5,16,129,16]{3,2,1,0:T(8,128)} %reshape.132), kind=kOutput, calls=%fused_computation | convolution fusion | flops 125829120 | bytes 7868416 | tf_op jit(solution)/shard_map/akbl,lp->akpb/dot_general | solution.py:48
  30.4 5.8 %add_bitcast_fusion = f32[5,16,64,128]{3,2,1,0:T(8,128)S(1)} fusion(f32[64,5,16,128]{3,0,2,1:T(8,128)S(1)} %fusion, f32[5,16,129,16]{3,2,1,0:T(8,128)S(1)} %copy-done, f32[32,32]{1,0:T(8,128)S(1)} %get-tuple-element.40, f32[32,32]{1,0:T(8,128)S(1)} %get-tuple-element.41), kind=kOutput, calls=%fused_computation.12 | convolution fusion | flops 126485504 | bytes 10518528 | tf_op jit(solution)/shard_map/akbl,lp->akpb/dot_general | solution.py:45
  36.8 1.2 copy.29
  38.1 1.2 copy.30
  39.3 4.2 %fusion.4 = f32[4,32,128,64,1,1]{2,3,5,4,1,0:T(8,128)S(1)} fusion(f32[4,1,16,2,32,128]{5,2,3,1,4,0:T(8,128)S(1)} %copy.30, f32[4,1,16,2,32,128]{5,2,3,1,4,0:T(8,128)S(1)} %copy.29, f32[64,2,16,2]{0,2,3,1:T(8,128)S(1)} %maximum_maximum_fusion), kind=kOutput, calls=%fused_computation.4 | convolution fusion | flops 806354944 | bytes 8404992 | tf_op jit(solution)/shard_map/tm,amvb->atvb/dot_general | solution.py:55
  43.5 4.4 %fusion.11 = f32[4,64,32,128]{3,1,2,0:T(8,128)S(1)} fusion(f32[64,64,1,1]{0,1,3,2:T(8,128)S(1)} %bitcast.75, f32[4,32,128,64,1,1]{2,3,5,4,1,0:T(8,128)S(1)} %fusion.4, f32[4,128]{1,0:T(4,128)S(1)} %copy-done.4, f32[64,32]{0,1:T(8,128)S(1)} %copy.31), kind=kOutput, calls=%fused_computation.13 | convolution fusion | flops 807403520 | bytes 8415232 | tf_op jit(solution)/shard_map/tm,atvb->amvb/dot_general | solution.py:66
  47.9 2.4 %copy.33 = f32[4,64,32,128]{3,2,1,0:T(8,128)S(1)} copy(f32[4,64,32,128]{3,1,2,0:T(8,128)S(1)} %fusion.11) | data formatting | bytes 8388608 | tf_op jit(solution)/shard_map/tm,atvb->amvb/transpose | solution.py:66
  50.9 1.5 fusion.18
  52.4 1.5 fusion.19
  55.5 3.4 %collective-permute-start.2 = (f32[16,2064]{1,0:T(8,128)}, f32[16,2064]{1,0:T(8,128)}, u32[]{:S(2)}, u32[]{:S(2)}) collective-permute-start(f32[16,2064]{1,0:T(8,128)} %slice.74), channel_id=1, source_target_pairs={{0,64},{64,128},{128,192},{1,65},{65,129},{129,193},{2,66},{66,130... | collective-permute-start | bytes 396296 | tf_op jit(solution)/shard_map/ppermute | solution.py:16
  59.6 1.1 pad_add_fusion.3
  60.8 2.1 %copy.37 = f32[3,16,129,16]{3,2,1,0:T(8,128)S(1)} copy(f32[3,16,129,16]{2,3,1,0:T(8,128)} %pad_add_fusion.3) | data formatting | bytes 792576 | tf_op jit(solution)/shard_map/slice | solution.py:89
  62.9 1.6 slice.76
  64.5 1.0 add.58
  66.3 3.8 %collective-permute-start.3 = (f32[64,16]{1,0:T(8,128)S(1)}, f32[64,16]{1,0:T(8,128)S(1)}, u32[]{:S(2)}, u32[]{:S(2)}) collective-permute-start(f32[64,16]{1,0:T(8,128)S(1)} %pad_maximum_fusion.1), channel_id=1, source_target_pairs={{0,1},{1,2},{2,3},{3,4},{4,5},{5,6},{6,7},{7,8},{8,9},{9,10},{10,1... | collective-permute-start | bytes 12296 | tf_op jit(solution)/shard_map/ppermute | solution.py:16
  71.9 2.1 %multiply_reduce_fusion = (f32[]{:T(128)}, f32[]{:T(128)}, f32[]{:T(128)}, f32[]{:T(128)}, f32[64,2048]{1,0:T(8,128)S(1)}) fusion(f32[64,2048]{1,0:T(8,128)} %param.6, f32[64,2048]{1,0:T(8,128)} %param.7, f32[48,2064]{1,0:T(8,128)} %slice.76, f32[16,2064]{1,0:T(8,128)S(1)} %add.58, f32[64,16]{1,0:T(8,128)S(1)} %maximum_add_fusion), kind=kLoop, calls=%fused_computation.27 | loop fusion | flops 1966076 | bytes 2105360 | tf_op jit(solution)/shard_map/reduce_sum | solution.py:99
  74.0 1.4 dynamic-update-slice.10
  75.5 1.4 dynamic-update-slice.15
  76.9 1.4 dynamic-update-slice.5
  78.3 1.4 dynamic-update-slice
  80.3 6.7 %all-reduce.26 = (f32[4]{0:T(128)S(1)}, f32[4]{0:T(128)S(1)}, f32[4]{0:T(128)S(1)}, f32[4]{0:T(128)S(1)}) all-reduce(f32[4]{0:T(128)S(1)} %dynamic-update-slice, f32[4]{0:T(128)S(1)} %dynamic-update-slice.5, f32[4]{0:T(128)S(1)} %dynamic-update-slice.10, ...), channel_id=1, replica_groups=mesh['row'=4,'col_0'=4,'col_1'=4,'col_2'=2,'col_3'=2] {'row'}, use_global_device_ids=true, to_apply=%add.4 | all-reduce | flops 16 | bytes 128
  88.2 1.4 dynamic-update-slice.11
  89.6 1.4 dynamic-update-slice.16
  91.6 1.4 dynamic-update-slice.6
  93.6 1.4 dynamic-update-slice.1
  95.6 10.6 %all-reduce.25 = (f32[4]{0:T(128)S(1)}, f32[4]{0:T(128)S(1)}, f32[4]{0:T(128)S(1)}, f32[4]{0:T(128)S(1)}) all-reduce(f32[4]{0:T(128)S(1)} %dynamic-update-slice.1, f32[4]{0:T(128)S(1)} %dynamic-update-slice.6, f32[4]{0:T(128)S(1)} %dynamic-update-slice.11, ...), channel_id=1, replica_groups=mesh['row'=4,'col_0'=4,'col_1'=4,'col_2'=2,'col_3'=2] {'col_0'}, use_global_device_ids=true, to_apply=%add.5 | all-reduce | flops 16 | bytes 128
  107.4 1.4 dynamic-update-slice.12
  108.8 1.4 dynamic-update-slice.17
  110.8 1.4 dynamic-update-slice.7
  112.8 1.4 dynamic-update-slice.2
  114.8 7.8 %all-reduce.24 = (f32[4]{0:T(128)S(1)}, f32[4]{0:T(128)S(1)}, f32[4]{0:T(128)S(1)}, f32[4]{0:T(128)S(1)}) all-reduce(f32[4]{0:T(128)S(1)} %dynamic-update-slice.2, f32[4]{0:T(128)S(1)} %dynamic-update-slice.7, f32[4]{0:T(128)S(1)} %dynamic-update-slice.12, ...), channel_id=1, replica_groups=mesh['row'=4,'col_0'=4,'col_1'=4,'col_2'=2,'col_3'=2] {'col_1'}, use_global_device_ids=true, to_apply=%add.6 | all-reduce | flops 16 | bytes 128
  123.8 1.4 dynamic-update-slice.13
  125.2 1.4 dynamic-update-slice.18
  127.2 1.4 dynamic-update-slice.8
  129.2 1.4 dynamic-update-slice.3
  131.2 7.7 %all-reduce.28 = (f32[2]{0:T(128)S(1)}, f32[2]{0:T(128)S(1)}, f32[2]{0:T(128)S(1)}, f32[2]{0:T(128)S(1)}) all-reduce(f32[2]{0:T(128)S(1)} %dynamic-update-slice.3, f32[2]{0:T(128)S(1)} %dynamic-update-slice.8, f32[2]{0:T(128)S(1)} %dynamic-update-slice.13, ...), channel_id=1, replica_groups=mesh['row'=4,'col_0'=4,'col_1'=4,'col_2'=2,'col_3'=2] {'col_2'}, use_global_device_ids=true, to_apply=%add.7 | all-reduce | flops 8 | bytes 64
  140.1 1.4 dynamic-update-slice.14
  141.5 1.4 dynamic-update-slice.19
  143.5 1.4 dynamic-update-slice.9
  145.5 1.4 dynamic-update-slice.4
  146.9 16.7 %all-reduce.27 = (f32[2]{0:T(128)S(1)}, f32[2]{0:T(128)S(1)}, f32[2]{0:T(128)S(1)}, f32[2]{0:T(128)S(1)}) all-reduce(f32[2]{0:T(128)S(1)} %dynamic-update-slice.4, f32[2]{0:T(128)S(1)} %dynamic-update-slice.9, f32[2]{0:T(128)S(1)} %dynamic-update-slice.14, ...), channel_id=1, replica_groups=mesh['row'=4,'col_0'=4,'col_1'=4,'col_2'=2,'col_3'=2] {'col_3'}, use_global_device_ids=true, to_apply=%add.8 | all-reduce | flops 8 | bytes 64
  170.0 1.3 multiply_add_fusion
  (89 shorter events, 22.5 us)
Async XLA Ops:
  1.4 11.8 %collective-permute-start = (f32[64,16]{1,0:T(8,128)S(1)}, f32[64,16]{1,0:T(8,128)S(1)}, u32[]{:S(2)}, u32[]{:S(2)}) collective-permute-start(f32[64,16]{1,0:T(8,128)S(1)} %slice.62), channel_id=1, source_target_pairs={{1,0},{2,1},{3,2},{4,3},{5,4},{6,5},{7,6},{8,7},{9,8},{10,9},{11,1... | collective-permute-start | bytes 12296 | tf_op jit(solution)/shard_map/ppermute | solution.py:16
  13.2 5.8 %collective-permute-start.1 = (f32[16,2064]{1,0:T(8,128)S(1)}, f32[16,2064]{1,0:T(8,128)S(1)}, u32[]{:S(2)}, u32[]{:S(2)}) collective-permute-start(f32[16,2064]{1,0:T(8,128)S(1)} %slice.82), channel_id=1, source_target_pairs={{64,0},{128,64},{192,128},{65,1},{129,65},{193,129},{66,2},{130,66... | collective-permute-start | bytes 396296 | tf_op jit(solution)/shard_map/ppermute | solution.py:16
  22.3 8.1 %copy-start = (f32[5,16,129,16]{3,2,1,0:T(8,128)S(1)}, f32[5,16,129,16]{3,2,1,0:T(8,128)}, u32[]{:S(2)}) copy-start(f32[5,16,129,16]{3,2,1,0:T(8,128)} %reshape.132) | copy-start | bytes 1981444
  39.3 4.2 %copy-start.4 = (f32[4,128]{1,0:T(4,128)S(1)}, f32[4,128]{1,0:T(4,128)}, u32[]{:S(2)}) copy-start(f32[4,128]{1,0:T(4,128)} %param.8) | copy-start | bytes 6148
  55.5 9.0 %collective-permute-start.2 = (f32[16,2064]{1,0:T(8,128)}, f32[16,2064]{1,0:T(8,128)}, u32[]{:S(2)}, u32[]{:S(2)}) collective-permute-start(f32[16,2064]{1,0:T(8,128)} %slice.74), channel_id=1, source_target_pairs={{0,64},{64,128},{128,192},{1,65},{65,129},{129,193},{2,66},{66,130... | collective-permute-start | bytes 396296 | tf_op jit(solution)/shard_map/ppermute | solution.py:16
  62.9 7.3 %copy-start.9 = (u32[256]{0:T(256)S(1)}, u32[256]{0:T(256)}, u32[]{:S(2)}) copy-start(u32[256]{0:T(256)} %constant.40) | copy-start | bytes 3076
  64.5 15.2 %copy-start.8 = (u32[256]{0:T(256)S(1)}, u32[256]{0:T(256)}, u32[]{:S(2)}) copy-start(u32[256]{0:T(256)} %constant.45) | copy-start | bytes 3076
  64.5 30.5 %copy-start.7 = (u32[256]{0:T(256)S(1)}, u32[256]{0:T(256)}, u32[]{:S(2)}) copy-start(u32[256]{0:T(256)} %constant.50) | copy-start | bytes 3076
  64.5 49.7 %copy-start.6 = (u32[256]{0:T(256)S(1)}, u32[256]{0:T(256)}, u32[]{:S(2)}) copy-start(u32[256]{0:T(256)} %constant.55) | copy-start | bytes 3076
  64.5 66.1 %copy-start.5 = (u32[256]{0:T(256)S(1)}, u32[256]{0:T(256)}, u32[]{:S(2)}) copy-start(u32[256]{0:T(256)} %constant.60) | copy-start | bytes 3076
  64.5 105.5 %copy-start.1 = (f32[64,2048]{1,0:T(8,128)S(1)}, f32[64,2048]{1,0:T(8,128)}, u32[]{:S(2)}) copy-start(f32[64,2048]{1,0:T(8,128)} %param.7) | copy-start | bytes 1572868
  64.5 105.5 %copy-start.2 = (f32[64,2048]{1,0:T(8,128)S(1)}, f32[64,2048]{1,0:T(8,128)}, u32[]{:S(2)}) copy-start(f32[64,2048]{1,0:T(8,128)} %param.6) | copy-start | bytes 1572868
  64.5 105.5 %copy-start.3 = (f32[64,2048]{1,0:T(8,128)S(1)}, f32[64,2048]{1,0:T(8,128)}, u32[]{:S(2)}) copy-start(f32[64,2048]{1,0:T(8,128)} %param.5) | copy-start | bytes 1572868
  66.3 4.8 %collective-permute-start.3 = (f32[64,16]{1,0:T(8,128)S(1)}, f32[64,16]{1,0:T(8,128)S(1)}, u32[]{:S(2)}, u32[]{:S(2)}) collective-permute-start(f32[64,16]{1,0:T(8,128)S(1)} %pad_maximum_fusion.1), channel_id=1, source_target_pairs={{0,1},{1,2},{2,3},{3,4},{4,5},{5,6},{6,7},{7,8},{8,9},{9,10},{10,1... | collective-permute-start | bytes 12296 | tf_op jit(solution)/shard_map/ppermute | solution.py:16
